TPU v7x, 32 devices: a whole 2x2x4 slice. The times are simulated.
32 devices in a mesh: seq: 8 (over y, x, core), rep: 4 (over z).
Axes of the slice: x: 2, y: 2, z: 4, core: 2. Of those that a mesh axis runs over, the one named last changes fastest.
Arguments:
- out_grad: bfloat16 [4, 16, 131072], P('rep', None, 'seq'), may hold values from -6 to 6
- gate_act: bfloat16 [4, 16, 131072], P('rep', None, 'seq'), may hold values from -6 to 6
- conv_out: bfloat16 [4, 16, 131072], P('rep', None, 'seq'), may hold values from -6 to 6
- value_act: bfloat16 [4, 16, 131072], P('rep', None, 'seq'), may hold values from -6 to 6
- filter_taps: float32 [131072], P('seq'), may hold values from -1 to 1
- skip_gain: float32 [16], replicated, may hold values from 0.25 to 1.75
Outputs:
- gate_grad: bfloat16 [4, 16, 131072], P('rep', None, 'seq')
- value_grad: bfloat16 [4, 16, 131072], P('rep', None, 'seq')
- filter_grad: float32 [131072], P('seq')
All inputs are finite; a program needn't handle non-finite values.
Results may differ from a plain program's by a relative error of at most 0.001.
Values sent between devices are 32-bit elements; how exact they have to be, the bound alone decides.
No kernel may reach another device: no remote copies, remote signals or barrier semaphores. Data moves between devices by JAX's collectives and lax.ppermute only.
A program may use at most 128 MiB of HBM per device.

v0:
```python
import math
import jax
import jax.numpy as jnp
from jax import lax
from jax.sharding import PartitionSpec as P

HIGHEST = lax.Precision.HIGHEST


def unit_table(product, modulus):
    phase_rad = (product % modulus).astype(jnp.float32) * (-2.0 * math.pi / modulus)
    return (jnp.cos(phase_rad), jnp.sin(phase_rad))


def middle_mix(table, values):
    lead_dims = values.shape[:-2]
    flat = values.reshape((-1,) + values.shape[-2:])
    tiled = jnp.broadcast_to(table[None], (flat.shape[0],) + table.shape)
    result = jnp.einsum("rka,rab->rkb", tiled, flat, precision=HIGHEST)
    return result.reshape(lead_dims + result.shape[-2:])


def middle_complex(left_re, left_im, table_re, table_im):
    out_re = middle_mix(table_re, left_re) - middle_mix(table_im, left_im)
    out_im = middle_mix(table_im, left_re) + middle_mix(table_re, left_im)
    return (out_re, out_im)


def last_complex(form, left_re, left_im, table_re, table_im):
    out_re = jnp.einsum(form, left_re, table_re, precision=HIGHEST) - jnp.einsum(
        form, left_im, table_im, precision=HIGHEST
    )
    out_im = jnp.einsum(form, left_re, table_im, precision=HIGHEST) + jnp.einsum(
        form, left_im, table_re, precision=HIGHEST
    )
    return (out_re, out_im)


def row_order(seq_count):
    slot_ids = jnp.arange(2 * seq_count, dtype=jnp.int32)
    owner_dev = slot_ids // 2
    second = jnp.where(owner_dev == 0, seq_count, 2 * seq_count - owner_dev)
    return jnp.where(slot_ids % 2 == 0, owner_dev, second)


def cross_forward(pieces):
    seq_count = pieces.shape[1]
    block_len = pieces.shape[2]
    modulus = 2 * seq_count * seq_count * block_len
    freq_rows = row_order(seq_count)
    sources = jnp.arange(seq_count, dtype=jnp.int32)
    table_re, table_im = unit_table(freq_rows[:, None] * sources[None, :], 2 * seq_count)
    mixed_re = middle_mix(table_re, pieces)
    mixed_im = middle_mix(table_im, pieces)
    offsets = lax.axis_index("seq") * block_len + jnp.arange(block_len, dtype=jnp.int32)
    twist_re, twist_im = unit_table(freq_rows[:, None] * offsets[None, :], modulus)
    return (mixed_re * twist_re - mixed_im * twist_im, mixed_re * twist_im + mixed_im * twist_re)


def cross_inverse(operands):
    re_part, im_part = operands
    seq_count = re_part.shape[1] // 2
    block_len = re_part.shape[2]
    modulus = 2 * seq_count * seq_count * block_len
    freq_rows = row_order(seq_count)
    offsets = lax.axis_index("seq") * block_len + jnp.arange(block_len, dtype=jnp.int32)
    twist_re, twist_im = unit_table(freq_rows[:, None] * offsets[None, :], modulus)
    re_part, im_part = (
        re_part * twist_re + im_part * twist_im,
        im_part * twist_re - re_part * twist_im,
    )
    sources = jnp.arange(seq_count, dtype=jnp.int32)
    table_re, table_im = unit_table(sources[:, None] * freq_rows[None, :], 2 * seq_count)
    out_re = middle_mix(table_re, re_part) + middle_mix(table_im, im_part)
    return out_re


def local_forward(operands):
    re_part, im_part = operands
    lead_dims = re_part.shape[:-1]
    length_s = re_part.shape[-1]
    rows_a = length_s // 128
    re_part = re_part.reshape(lead_dims + (rows_a, 128))
    im_part = im_part.reshape(lead_dims + (rows_a, 128))
    steps_a = jnp.arange(rows_a, dtype=jnp.int32)
    steps_b = jnp.arange(128, dtype=jnp.int32)
    first_re, first_im = unit_table(steps_a[:, None] * steps_a[None, :], rows_a)
    re_part, im_part = middle_complex(re_part, im_part, first_re, first_im)
    twist_re, twist_im = unit_table(steps_a[:, None] * steps_b[None, :], length_s)
    re_part, im_part = (
        re_part * twist_re - im_part * twist_im,
        re_part * twist_im + im_part * twist_re,
    )
    last_re, last_im = unit_table(steps_b[:, None] * steps_b[None, :], 128)
    return last_complex("...kb,bl->...kl", re_part, im_part, last_re, last_im)


def local_inverse(re_part, im_part):
    lead_dims = re_part.shape[:-2]
    rows_a = re_part.shape[-2]
    length_s = rows_a * 128
    steps_a = jnp.arange(rows_a, dtype=jnp.int32)
    steps_b = jnp.arange(128, dtype=jnp.int32)
    last_re, last_im = unit_table(steps_b[:, None] * steps_b[None, :], 128)
    re_part, im_part = last_complex("...kl,bl->...kb", re_part, im_part, last_re, -last_im)
    twist_re, twist_im = unit_table(steps_a[:, None] * steps_b[None, :], length_s)
    re_part, im_part = (
        re_part * twist_re + im_part * twist_im,
        im_part * twist_re - re_part * twist_im,
    )
    first_re, first_im = unit_table(steps_a[:, None] * steps_a[None, :], rows_a)
    re_part, im_part = middle_complex(re_part, im_part, first_re, -first_im)
    return (re_part.reshape(lead_dims + (length_s,)), im_part.reshape(lead_dims + (length_s,)))


def local(out_grad, gate_act, conv_out, value_act, filter_taps, skip_gain):
    batch_rows = out_grad.shape[0]
    channels = out_grad.shape[1]
    length_s = out_grad.shape[2]
    seq_count = lax.axis_size("seq")
    row_total = batch_rows * channels
    gated_rows = out_grad.astype(jnp.float32) * gate_act.astype(jnp.float32)
    gate_grad = (out_grad.astype(jnp.float32) * conv_out.astype(jnp.float32)).astype(jnp.bfloat16)
    stacked = jnp.concatenate(
        [
            gated_rows.reshape(row_total, length_s),
            value_act.astype(jnp.float32).reshape(row_total, length_s),
            filter_taps.reshape(1, length_s),
        ],
        axis=0,
    )
    mixed_re, mixed_im = cross_forward(
        lax.all_to_all(
            stacked.reshape(2 * row_total + 1, 1, length_s),
            "seq",
            split_axis=2,
            concat_axis=1,
            tiled=True,
        )
    )
    spec_re, spec_im = local_forward(
        (
            lax.all_to_all(mixed_re, "seq", split_axis=1, concat_axis=2, tiled=True),
            lax.all_to_all(mixed_im, "seq", split_axis=1, concat_axis=2, tiled=True),
        )
    )
    grad_re = spec_re[:row_total]
    grad_im = spec_im[:row_total]
    value_re = spec_re[row_total : 2 * row_total]
    value_im = spec_im[row_total : 2 * row_total]
    filt_re = spec_re[2 * row_total]
    filt_im = spec_im[2 * row_total]
    carry_re = filt_re * grad_re + filt_im * grad_im
    carry_im = filt_re * grad_im - filt_im * grad_re
    lag_re = jnp.sum(grad_re * value_re + grad_im * value_im, axis=0)
    lag_im = jnp.sum(grad_im * value_re - grad_re * value_im, axis=0)
    lag_re, lag_im = lax.psum((lag_re, lag_im), "rep")
    back_re, back_im = local_inverse(
        jnp.concatenate([carry_re, lag_re[None]], axis=0),
        jnp.concatenate([carry_im, lag_im[None]], axis=0),
    )
    rows_out = cross_inverse(
        (
            lax.all_to_all(back_re, "seq", split_axis=2, concat_axis=1, tiled=True),
            lax.all_to_all(back_im, "seq", split_axis=2, concat_axis=1, tiled=True),
        )
    )
    rows_time = lax.all_to_all(rows_out, "seq", split_axis=1, concat_axis=2, tiled=True)
    rows_time = rows_time.reshape(row_total + 1, length_s) * (1.0 / (2 * seq_count * length_s))
    carried = rows_time[:row_total].reshape(batch_rows, channels, length_s)
    value_grad = (carried + skip_gain[None, :, None] * gated_rows).astype(jnp.bfloat16)
    lag_taps = rows_time[row_total]
    norm_scale = 1.0 / math.sqrt(
        batch_rows * lax.axis_size("rep") * channels * length_s * seq_count
    )
    filter_grad = lag_taps * norm_scale
    return (gate_grad, value_grad, filter_grad)


def solution(mesh):
    return jax.shard_map(
        local,
        mesh=mesh,
        in_specs=(
            P("rep", None, "seq"),
            P("rep", None, "seq"),
            P("rep", None, "seq"),
            P("rep", None, "seq"),
            P("seq"),
            P(),
        ),
        out_specs=(P("rep", None, "seq"), P("rep", None, "seq"), P("seq")),
        check_vma=False,
    )
```

profile of v0, /device:TPU:0, one launch (start us, length us, event | category | flops | bytes accessed | tf_op | source)
XLA Modules:
  0.0 709.1 jit_solution(3196688340106611680)
XLA Ops:
  9.8 4.8 copy.63
  15.1 74.5 %reduce = f32[16384,33]{1,0:T(8,128)} reduce(f32[16384,1,33]{2,1,0:T(1,128)} %bitcast.95, f32[]{:T(128)} %broadcast.616), dimensions={1}, to_apply=%bitcast.60.reduce_sub_computation | reduce | bytes 4325380
  89.6 11.2 %reshape.394 = f32[8,1,67584]{2,1,0:T(1,128)} reshape(f32[16384,33]{1,0:T(8,128)} %reduce) | data formatting | bytes 4325376
  100.7 5.3 all-to-all-start
  106.8 26.6 %all-to-all-done = f32[8,1,67584]{2,1,0:T(1,128)} async-done(((f32[8,1,67584]{2,1,0:T(1,128)}), f32[8,1,67584]{2,1,0:T(1,128)}, u32[]{:S(2)}, u32[]{:S(2)}) %all-to-all-start) | async-done | bytes 2162720 | tf_op jit(solution)/shard_map/all_to_all | solution.py:133
  133.4 7.4 %reduce.1 = f32[8,67584]{1,0:T(8,128)S(1)} reduce(f32[8,1,67584]{2,1,0:T(1,128)} %all-to-all-done, f32[]{:T(128)} %broadcast.616), dimensions={1}, to_apply=%all_to_all.64.reduce_sub_computation | reduce | bytes 4325380 | tf_op jit(solution)/shard_map/all_to_all | solution.py:133
  140.8 20.0 %reshape.395 = f32[16384,1,33]{2,1,0:T(1,128)} reshape(f32[8,67584]{1,0:T(8,128)S(1)} %reduce.1) | data formatting | bytes 4325376
  160.7 5.5 copy.78
  170.1 6.4 multiply_add_fusion.1
  176.5 4.9 copy.67
  186.1 7.1 %copy.65 = f32[33,16,2048]{2,0,1:T(8,128)} copy(f32[33,16,2048]{2,1,0:T(8,128)} %get-tuple-element.16) | data formatting | bytes 8650752 | tf_op jit(solution)/shard_map/sub | solution.py:57
  193.2 53.3 %all-to-all-done.2 = f32[33,16,2048]{2,0,1:T(8,128)} async-done(((f32[33,16,2048]{2,0,1:T(8,128)}), f32[33,16,2048]{2,0,1:T(8,128)}, u32[]{:S(2)}, u32[]{:S(2)}) %all-to-all-start.2) | async-done | bytes 4325408 | tf_op jit(solution)/shard_map/all_to_all | solution.py:144
  246.4 4.7 all-to-all-start.1
  252.0 7.0 copy.81
  259.0 5.3 reshape_reshape.9
  264.3 47.2 %all-to-all-done.1 = f32[33,16,2048]{2,0,1:T(8,128)} async-done(((f32[33,16,2048]{2,0,1:T(8,128)}), f32[33,16,2048]{2,0,1:T(8,128)}, u32[]{:S(2)}, u32[]{:S(2)}) %all-to-all-start.1) | async-done | bytes 4325408 | tf_op jit(solution)/shard_map/all_to_all | solution.py:143
  311.5 7.0 copy.82
  318.5 5.3 reshape_reshape.8
  323.8 6.2 fusion.7
  339.1 4.8 convolution_add_fusion.2
  364.6 35.4 %all-reduce.3.cloned.1.call-done = (f32[1,2,128,128]{3,2,1,0:T(8,128)}, f32[1,2,128,128]{3,2,1,0:T(8,128)}) async-done(((f32[1,2,128,128]{3,2,1,0:T(8,128)}, f32[1,2,128,128]{3,2,1,0:T(8,128)}), (f32[1,2,128,128]{3,2,1,0:T(8,128)}, f32[1,2,128,128]{3,2,1,0:T(8,128)})) %all-reduce.3.cloned.1.call-update) | async-done | bytes 262160 | tf_op jit(solution)/shard_map/psum | solution.py:157
  422.7 18.8 %copy.71 = f32[17,2,16384]{0,1,2:T(2,128)} copy(f32[17,2,16384]{2,1,0:T(2,128)} %add.234) | data formatting | bytes 4456448 | tf_op jit(solution)/shard_map/add | solution.py:25
  441.5 27.5 %reshape.396 = f32[8,1,69632]{2,1,0:T(1,128)} reshape(f32[16384,2,17]{2,1,0:T(2,128)} %bitcast.88) | data formatting | bytes 4456448
  483.7 15.1 %copy.69 = f32[17,2,16384]{0,1,2:T(2,128)} copy(f32[17,2,16384]{2,1,0:T(2,128)S(1)} %sub.82) | data formatting | bytes 4456448 | tf_op jit(solution)/shard_map/sub | solution.py:24
  498.8 27.5 %reshape.398 = f32[8,1,69632]{2,1,0:T(1,128)} reshape(f32[16384,2,17]{2,1,0:T(2,128)} %bitcast.89) | data formatting | bytes 4456448
  530.9 7.6 %reduce.2 = f32[8,69632]{1,0:T(8,128)S(1)} reduce(f32[8,1,69632]{2,1,0:T(1,128)} %all-to-all-done.4, f32[]{:T(128)} %broadcast.616), dimensions={1}, to_apply=%all_to_all.76.reduce_sub_computation | reduce | bytes 4456452 | tf_op jit(solution)/shard_map/all_to_all | solution.py:165
  538.5 32.8 %reshape.397 = f32[16384,2,17]{2,1,0:T(2,128)} reshape(f32[8,69632]{1,0:T(8,128)S(1)} %reduce.2) | data formatting | bytes 4456448
  571.3 22.0 %copy.72 = f32[17,8,2,2048]{3,2,1,0:T(2,128)} copy(f32[17,8,2,2048]{0,2,3,1:T(2,128)} %bitcast.90) | data formatting | bytes 4456448 | tf_op jit(solution)/shard_map/all_to_all | solution.py:165
  596.4 8.9 %reduce.3 = f32[8,69632]{1,0:T(8,128)} reduce(f32[8,1,69632]{2,1,0:T(1,128)} %all-to-all-done.3, f32[]{:T(128)} %broadcast.616), dimensions={1}, to_apply=%all_to_all.72.reduce_sub_computation | reduce | bytes 4456452 | tf_op jit(solution)/shard_map/all_to_all | solution.py:164
  605.4 35.9 %reshape.399 = f32[16384,2,17]{2,1,0:T(2,128)} reshape(f32[8,69632]{1,0:T(8,128)} %reduce.3) | data formatting | bytes 4456448
  641.2 22.0 %copy.70 = f32[17,8,2,2048]{3,2,1,0:T(2,128)} copy(f32[17,8,2,2048]{0,2,3,1:T(2,128)} %bitcast.91) | data formatting | bytes 4456448 | tf_op jit(solution)/shard_map/all_to_all | solution.py:164
  672.6 24.9 %all_to_all.87 = f32[17,8,2048]{2,0,1:T(8,128)S(1)} all-to-all(f32[17,8,2048]{2,0,1:T(8,128)S(1)} %copy.73), channel_id=1, replica_groups=mesh['seq'=8,'rep'=4] {'seq'}, dimensions={1} | all-to-all | bytes 2228224 | tf_op jit(solution)/shard_map/all_to_all | solution.py:168
  (78 shorter events, 101.6 us)
Async XLA Ops:
  7.2 2.5 copy-start.9
  100.7 32.6 %all-to-all-start = ((f32[8,1,67584]{2,1,0:T(1,128)}), f32[8,1,67584]{2,1,0:T(1,128)}, u32[]{:S(2)}, u32[]{:S(2)}) async-start(f32[8,1,67584]{2,1,0:T(1,128)} %reshape.394), calls=%async_computation | async-start | bytes 4325376 | tf_op jit(solution)/shard_map/all_to_all | solution.py:133
  181.4 65.0 %all-to-all-start.2 = ((f32[33,16,2048]{2,0,1:T(8,128)}), f32[33,16,2048]{2,0,1:T(8,128)}, u32[]{:S(2)}, u32[]{:S(2)}) async-start(f32[33,16,2048]{2,0,1:T(8,128)} %copy.67), calls=%async_computation.2 | async-start | bytes 10485760 | tf_op jit(solution)/shard_map/all_to_all | solution.py:144
  246.4 65.0 %all-to-all-start.1 = ((f32[33,16,2048]{2,0,1:T(8,128)}), f32[33,16,2048]{2,0,1:T(8,128)}, u32[]{:S(2)}, u32[]{:S(2)}) async-start(f32[33,16,2048]{2,0,1:T(8,128)} %copy.65), calls=%async_computation.1 | async-start | bytes 10485760 | tf_op jit(solution)/shard_map/all_to_all | solution.py:143
  251.1 148.8 %all-reduce.3.cloned.1.call-start = ((), (), s32[]{:S(2)}) async-start(), calls=%async_computation.6 | async-start | bytes 524288 | tf_op jit(solution)/shard_map/psum | solution.py:157
  323.8 6.2 copy-start
  323.8 10.7 %slice-start = ((s8[4325376]{0:T(1024)(128)(4,1)}), s8[4194304]{0:T(1024)(128)(4,1)S(1)}, s32[]{:S(2)}) async-start(s8[4325376]{0:T(1024)(128)(4,1)} %bitcast.92), calls=%async_computation.7 | async-start | bytes 8388608
  330.0 4.5 slice-start.1
  364.3 41.9 %copy-start.3 = (f32[16,2,128,128]{3,2,1,0:T(8,128)}, f32[16,2,128,128]{3,2,1,0:T(8,128)S(1)}, u32[]{:S(2)}) copy-start(f32[16,2,128,128]{3,2,1,0:T(8,128)S(1)} %get-tuple-element.13) | copy-start | bytes 6291460
  400.0 4.0 copy-start.4
  400.0 4.0 copy-start.8
  404.0 2.2 copy-start.7
  413.2 2.2 copy-start.2
  469.0 57.3 %all-to-all-start.4 = ((f32[8,1,69632]{2,1,0:T(1,128)}), f32[8,1,69632]{2,1,0:T(1,128)}, u32[]{:S(2)}, u32[]{:S(2)}) async-start(f32[8,1,69632]{2,1,0:T(1,128)} %reshape.396), calls=%async_computation.4 | async-start | bytes 4456448 | tf_op jit(solution)/shard_map/all_to_all | solution.py:165
  526.3 70.1 %all-to-all-start.3 = ((f32[8,1,69632]{2,1,0:T(1,128)}), f32[8,1,69632]{2,1,0:T(1,128)}, u32[]{:S(2)}, u32[]{:S(2)}) async-start(f32[8,1,69632]{2,1,0:T(1,128)} %reshape.398), calls=%async_computation.3 | async-start | bytes 4456448 | tf_op jit(solution)/shard_map/all_to_all | solution.py:164
  667.2 3.2 copy-start.1
  698.5 1.0 copy-start.5
  698.5 1.2 copy-start.6
  698.5 1.2 copy-start.10
Sparse Core Ops, SparseCore 0:
  364.5 35.4 all-reduce.2
where the time goes:
time: 718 us; the launch traced here: 709 us
  local copies, waits for them, and re-layouts  296 us (41%)
  waiting for transfers between devices  162 us (23%)
  other arithmetic  109 us (15%)
  matrix products  78.3 us (11%)
  blocking collectives  24.9 us (3%)
  starting transfers between devices  23.8 us (3%)
  between operations  14.8 us (2%)
    unnamed x33, local copies, waits for them, and re-layouts  156 us
    unnamed x2, other arithmetic  74.5 us
    all_to_all x1, waiting for transfers between devices, local(): lax.all_to_all(mixed_im, 'seq', split_axis=1, concat_axis=2, tiled=True)  53.3 us
    dot_general x12, matrix products, middle_mix(): result = jnp.einsum('rka,rab->rkb', tiled, flat, precision=HIGHEST)  48 us
    all_to_all x1, waiting for transfers between devices, local(): lax.all_to_all(mixed_re, 'seq', split_axis=1, concat_axis=2, tiled=True)  47.2 us
    psum x1, waiting for transfers between devices, local(): lag_re, lag_im = lax.psum((lag_re, lag_im), 'rep')  35.4 us
    all_to_all x1, waiting for transfers between devices, local(): lax.all_to_all(stacked.reshape(2 * row_total + 1, 1, length_s), 'seq', sp...  26.6 us
    all_to_all x2, local copies, waits for them, and re-layouts, local(): lax.all_to_all(back_re, 'seq', split_axis=2, concat_axis=1, tiled=True)  26 us
  transfers between devices with their start and end apart: 6, of which 4 were waited for; matrix products, arithmetic and copies ran while one was open for 19% of the time, Pallas kernels for 0%

commit v1 on v0

--- a/solution.py
+++ b/solution.py
@@ -162,7 +162,12 @@
     rows_out = cross_inverse(
         (
             lax.all_to_all(back_re, "seq", split_axis=2, concat_axis=1, tiled=True),
-            lax.all_to_all(back_im, "seq", split_axis=2, concat_axis=1, tiled=True),
+            jnp.concatenate(
+                lax.all_to_all(
+                    jnp.stack(jnp.split(back_im, lax.axis_size("seq"), axis=2)), "seq", 0, 0
+                ),
+                axis=1,
+            ),
         )
     )
     rows_time = lax.all_to_all(rows_out, "seq", split_axis=1, concat_axis=2, tiled=True)

time: 718 us -> 644 us (0.90)
  local copies, waits for them, and re-layouts: 296 us -> 213 us
  waiting for transfers between devices: 162 us -> 183 us
  other arithmetic: 109 us -> 101 us
    unnamed x33 -> x40, local copies, waits for them, and re-layouts: 156 us -> 107 us
    all_to_all x2 -> x0, local copies, waits for them, and re-layouts: 25.1 us -> none  [local(): lax.all_to_all(back_im, 'seq', split_axis=2, concat_axis=1, tiled=True)]
    all_to_all x1, waiting for transfers between devices: 0.01 us -> 20.6 us  [local(): lax.all_to_all(back_re, 'seq', split_axis=2, concat_axis=1, tiled=True)]
    add x2 -> x1, local copies, waits for them, and re-layouts: 22.5 us -> 3.66 us  [middle_complex(): out_im = middle_mix(table_im, left_re) + middle_mix(table_re, left_im)]
    all_to_all x1 -> x0, other arithmetic: 7.57 us -> none  [local(): lax.all_to_all(back_im, 'seq', split_axis=2, concat_axis=1, tiled=True)]
    reshape x0 -> x2, local copies, waits for them, and re-layouts: none -> 7.43 us  [local(): jnp.concatenate(lax.all_to_all(jnp.stack(jnp.split(back_im, lax.axis_size...]
    unnamed x2 -> x3, other arithmetic: 74.5 us -> 74.5 us
  transfers between devices with their start and end apart: 6 -> 6, of which waited for: 4 -> 5; matrix products, arithmetic and copies ran while one was open for 19% -> 13% of each run, Pallas kernels for 0% -> 0%
where the time goes in v1:
time: 644 us; the launch traced here: 637 us
  local copies, waits for them, and re-layouts  213 us (33%)
  waiting for transfers between devices  183 us (28%)
  other arithmetic  101 us (16%)
  matrix products  78.3 us (12%)
  starting transfers between devices  23.7 us (4%)
  blocking collectives  23.4 us (4%)
  between operations  14.7 us (2%)
    unnamed x40, local copies, waits for them, and re-layouts  107 us
    unnamed x3, other arithmetic  74.5 us
    all_to_all x1, waiting for transfers between devices, local(): lax.all_to_all(mixed_re, 'seq', split_axis=1, concat_axis=2, tiled=True)  53.2 us
    dot_general x12, matrix products, middle_mix(): result = jnp.einsum('rka,rab->rkb', tiled, flat, precision=HIGHEST)  47.9 us
    all_to_all x1, waiting for transfers between devices, local(): lax.all_to_all(mixed_im, 'seq', split_axis=1, concat_axis=2, tiled=True)  47.2 us
    psum x1, waiting for transfers between devices, local(): lag_re, lag_im = lax.psum((lag_re, lag_im), 'rep')  35.3 us
    all_to_all x1, waiting for transfers between devices, local(): lax.all_to_all(stacked.reshape(2 * row_total + 1, 1, length_s), 'seq', sp...  26.5 us
    all_to_all x2, local copies, waits for them, and re-layouts, local(): lax.all_to_all(back_re, 'seq', split_axis=2, concat_axis=1, tiled=True)  25.9 us
  transfers between devices with their start and end apart: 6, of which 5 were waited for; matrix products, arithmetic and copies ran while one was open for 13% of the time, Pallas kernels for 0%

profile of v1, /device:TPU:0, one launch (start us, length us, event | category | flops | bytes accessed | tf_op | source)
XLA Modules:
  0.0 637.0 jit_solution(2106435466900264622)
XLA Ops:
  9.8 4.8 copy.60
  15.1 74.5 %reduce = f32[16384,33]{1,0:T(8,128)} reduce(f32[16384,1,33]{2,1,0:T(1,128)} %bitcast.123, f32[]{:T(128)} %broadcast.616), dimensions={1}, to_apply=%bitcast.90.reduce_sub_computation | reduce | bytes 4325380
  89.6 11.2 %reshape.402 = f32[8,1,67584]{2,1,0:T(1,128)} reshape(f32[16384,33]{1,0:T(8,128)} %reduce) | data formatting | bytes 4325376
  100.8 5.4 all-to-all-start
  107.0 26.5 %all-to-all-done = f32[8,1,67584]{2,1,0:T(1,128)} async-done(((f32[8,1,67584]{2,1,0:T(1,128)}), f32[8,1,67584]{2,1,0:T(1,128)}, u32[]{:S(2)}, u32[]{:S(2)}) %all-to-all-start) | async-done | bytes 2162720 | tf_op jit(solution)/shard_map/all_to_all | solution.py:133
  133.4 7.4 %reduce.1 = f32[8,67584]{1,0:T(8,128)S(1)} reduce(f32[8,1,67584]{2,1,0:T(1,128)} %all-to-all-done, f32[]{:T(128)} %broadcast.616), dimensions={1}, to_apply=%all_to_all.54.reduce_sub_computation | reduce | bytes 4325380 | tf_op jit(solution)/shard_map/all_to_all | solution.py:133
  140.8 20.2 %reshape.403 = f32[16384,1,33]{2,1,0:T(1,128)} reshape(f32[8,67584]{1,0:T(8,128)S(1)} %reduce.1) | data formatting | bytes 4325376
  161.0 5.5 copy.74
  170.4 6.3 multiply_add_fusion.1
  176.7 4.9 copy.62
  181.7 4.7 all-to-all-start.1
  186.4 7.1 %copy.64 = f32[33,16,2048]{2,0,1:T(8,128)} copy(f32[33,16,2048]{2,1,0:T(8,128)} %get-tuple-element.15) | data formatting | bytes 8650752 | tf_op jit(solution)/shard_map/add | solution.py:57
  193.5 53.2 %all-to-all-done.1 = f32[33,16,2048]{2,0,1:T(8,128)} async-done(((f32[33,16,2048]{2,0,1:T(8,128)}), f32[33,16,2048]{2,0,1:T(8,128)}, u32[]{:S(2)}, u32[]{:S(2)}) %all-to-all-start.1) | async-done | bytes 4325408 | tf_op jit(solution)/shard_map/all_to_all | solution.py:143
  246.7 4.7 all-to-all-start.2
  252.2 7.0 %copy.78 = f32[33,8,2,2048]{3,1,2,0:T(8,128)} copy(f32[33,8,2,2048]{3,0,2,1:T(8,128)} %bitcast.5) | data formatting | bytes 8650752 | tf_op jit(solution)/shard_map/all_to_all | solution.py:143
  259.2 5.3 reshape_reshape.8
  264.5 47.2 %all-to-all-done.2 = f32[33,16,2048]{2,0,1:T(8,128)} async-done(((f32[33,16,2048]{2,0,1:T(8,128)}), f32[33,16,2048]{2,0,1:T(8,128)}, u32[]{:S(2)}, u32[]{:S(2)}) %all-to-all-start.2) | async-done | bytes 4325408 | tf_op jit(solution)/shard_map/all_to_all | solution.py:144
  311.7 7.0 %copy.77 = f32[33,8,2,2048]{3,1,2,0:T(8,128)} copy(f32[33,8,2,2048]{3,0,2,1:T(8,128)} %bitcast.7) | data formatting | bytes 8650752 | tf_op jit(solution)/shard_map/all_to_all | solution.py:144
  318.7 5.3 reshape_reshape.9
  324.1 6.2 fusion.7
  334.8 4.6 convolution_add_fusion.2
  339.4 4.8 convolution_subtract_fusion.1
  352.6 4.5 convolution_add_fusion.1
  364.8 35.3 %all-reduce.3.cloned.1.call-done = (f32[1,2,128,128]{3,2,1,0:T(8,128)}, f32[1,2,128,128]{3,2,1,0:T(8,128)}) async-done(((f32[1,2,128,128]{3,2,1,0:T(8,128)}, f32[1,2,128,128]{3,2,1,0:T(8,128)}), (f32[1,2,128,128]{3,2,1,0:T(8,128)}, f32[1,2,128,128]{3,2,1,0:T(8,128)})) %all-reduce.3.cloned.1.call-update) | async-done | bytes 262160 | tf_op jit(solution)/shard_map/psum | solution.py:157
  436.4 4.5 all-to-all-start.4
  451.1 15.1 %copy.66 = f32[17,2,16384]{0,1,2:T(2,128)} copy(f32[17,2,16384]{2,1,0:T(2,128)S(1)} %sub.82) | data formatting | bytes 4456448 | tf_op jit(solution)/shard_map/sub | solution.py:24
  466.2 27.5 %reshape.404 = f32[8,1,69632]{2,1,0:T(1,128)} reshape(f32[16384,2,17]{2,1,0:T(2,128)} %bitcast.116) | data formatting | bytes 4456448
  505.6 20.6 %all-to-all-done.3 = f32[8,1,69632]{2,1,0:T(1,128)} async-done(((f32[8,1,69632]{2,1,0:T(1,128)}), f32[8,1,69632]{2,1,0:T(1,128)}, u32[]{:S(2)}, u32[]{:S(2)}) %all-to-all-start.3) | async-done | bytes 2228256 | tf_op jit(solution)/shard_map/all_to_all | solution.py:164
  526.1 9.0 %reduce.2 = f32[8,69632]{1,0:T(8,128)} reduce(f32[8,1,69632]{2,1,0:T(1,128)} %all-to-all-done.3, f32[]{:T(128)} %broadcast.616), dimensions={1}, to_apply=%all_to_all.62.reduce_sub_computation | reduce | bytes 4456452 | tf_op jit(solution)/shard_map/all_to_all | solution.py:164
  535.1 36.0 %reshape.405 = f32[16384,2,17]{2,1,0:T(2,128)} reshape(f32[8,69632]{1,0:T(8,128)} %reduce.2) | data formatting | bytes 4456448
  571.1 22.0 %copy.67 = f32[17,8,2,2048]{3,2,1,0:T(2,128)} copy(f32[17,8,2,2048]{0,2,3,1:T(2,128)} %bitcast.117) | data formatting | bytes 4456448 | tf_op jit(solution)/shard_map/all_to_all | solution.py:164
  602.5 23.4 %all_to_all.74 = f32[17,8,2048]{2,0,1:T(8,128)S(1)} all-to-all(f32[17,8,2048]{2,0,1:T(8,128)S(1)} %copy.69), channel_id=1, replica_groups=mesh['seq'=8,'rep'=4] {'seq'}, dimensions={1} | all-to-all | bytes 2228224 | tf_op jit(solution)/shard_map/all_to_all | solution.py:173
  (85 shorter events, 100.4 us)
Async XLA Ops:
  7.2 2.5 copy-start.8
  100.8 32.6 %all-to-all-start = ((f32[8,1,67584]{2,1,0:T(1,128)}), f32[8,1,67584]{2,1,0:T(1,128)}, u32[]{:S(2)}, u32[]{:S(2)}) async-start(f32[8,1,67584]{2,1,0:T(1,128)} %reshape.402), calls=%async_computation | async-start | bytes 4325376 | tf_op jit(solution)/shard_map/all_to_all | solution.py:133
  181.7 65.0 %all-to-all-start.1 = ((f32[33,16,2048]{2,0,1:T(8,128)}), f32[33,16,2048]{2,0,1:T(8,128)}, u32[]{:S(2)}, u32[]{:S(2)}) async-start(f32[33,16,2048]{2,0,1:T(8,128)} %copy.62), calls=%async_computation.1 | async-start | bytes 10485760 | tf_op jit(solution)/shard_map/all_to_all | solution.py:143
  246.7 65.0 %all-to-all-start.2 = ((f32[33,16,2048]{2,0,1:T(8,128)}), f32[33,16,2048]{2,0,1:T(8,128)}, u32[]{:S(2)}, u32[]{:S(2)}) async-start(f32[33,16,2048]{2,0,1:T(8,128)} %copy.64), calls=%async_computation.2 | async-start | bytes 10485760 | tf_op jit(solution)/shard_map/all_to_all | solution.py:144
  251.4 148.8 %all-reduce.3.cloned.1.call-start = ((), (), s32[]{:S(2)}) async-start(), calls=%async_computation.6 | async-start | bytes 524288 | tf_op jit(solution)/shard_map/psum | solution.py:157
  318.7 11.6 %slice-start = ((s8[4325376]{0:T(1024)(128)(4,1)}), s8[131072]{0:T(1024)(128)(4,1)S(1)}, s32[]{:S(2)}) async-start(s8[4325376]{0:T(1024)(128)(4,1)} %bitcast.118), calls=%async_computation.7 | async-start | bytes 262144
  324.1 6.2 slice-start.1
  324.1 10.7 %slice-start.2 = ((s8[4325376]{0:T(1024)(128)(4,1)}), s8[4194304]{0:T(1024)(128)(4,1)S(1)}, s32[]{:S(2)}) async-start(s8[4325376]{0:T(1024)(128)(4,1)} %bitcast.120), calls=%async_computation.9 | async-start | bytes 8388608
  330.3 4.4 slice-start.3
  364.5 41.9 %copy-start.2 = (f32[16,2,128,128]{3,2,1,0:T(8,128)}, f32[16,2,128,128]{3,2,1,0:T(8,128)S(1)}, u32[]{:S(2)}) copy-start(f32[16,2,128,128]{3,2,1,0:T(8,128)S(1)} %get-tuple-element.13) | copy-start | bytes 6291460
  400.2 4.0 copy-start.3
  400.2 4.0 copy-start.7
  404.2 2.2 copy-start.6
  413.4 2.2 copy-start.1
  436.4 57.3 %all-to-all-start.4 = ((f32[8,17,2,2048]{3,2,1,0:T(2,128)}), f32[8,17,2,2048]{3,2,1,0:T(2,128)}, u32[]{:S(2)}, u32[]{:S(2)}) async-start(f32[8,17,2,2048]{3,2,1,0:T(2,128)} %fusion.33), calls=%async_computation.4 | async-start | bytes 4456448 | tf_op jit(solution)/shard_map/all_to_all | solution.py:166
  493.7 32.4 %all-to-all-start.3 = ((f32[8,1,69632]{2,1,0:T(1,128)}), f32[8,1,69632]{2,1,0:T(1,128)}, u32[]{:S(2)}, u32[]{:S(2)}) async-start(f32[8,1,69632]{2,1,0:T(1,128)} %reshape.404), calls=%async_computation.3 | async-start | bytes 4456448 | tf_op jit(solution)/shard_map/all_to_all | solution.py:164
  597.0 3.2 copy-start
  626.1 1.5 copy-start.4
  626.1 1.5 copy-start.5
  626.1 1.5 copy-start.9
Sparse Core Ops, SparseCore 0:
  364.7 35.4 all-reduce.2
